TPU v7x, 256 devices: a whole 4x4x8 slice. The times are simulated.
256 devices in a mesh: dp: 8 (over z), seq: 32 (over y, x, core).
Axes of the slice: x: 4, y: 4, z: 8, core: 2. Of those that a mesh axis runs over, the one named last changes fastest.
Arguments:
- inputs: bfloat16 [8, 4096, 2048], P('dp', 'seq'), may hold values from -6 to 6
- weight_codes: bfloat16 [2048, 1280], P('seq'), may hold values from -4 to 4
- scales: bfloat16 [2048, 10], P('seq'), may hold values from 0.010986328 to 0.043945312
- log_decay: float32 [8, 16, 4096], P('dp', None, 'seq'), may hold values from -0.85 to 0, as said below
- cotangent: bfloat16 [8, 4096, 1024], P('dp', 'seq'), may hold values from -6 to 6
Outputs:
- grad_inputs: float32 [8, 4096, 2048], P('dp', 'seq')
- grad_weight: float32 [2048, 1280], P('seq')
Inputs may be any that keep to these rules, and one draw needn't show every extreme that they name: log_decay is negative everywhere.
All inputs are finite; a program needn't handle non-finite values.
Results may differ from a plain program's by a relative error of at most 0.017.
Values may be sent and summed in bfloat16 or wider, within the bound.
No kernel may reach another device: no remote copies, remote signals or barrier semaphores. Data moves between devices by JAX's collectives and lax.ppermute only.
A program may use at most 128 MiB of HBM per device.

v0:
```python
import math
import jax
import jax.numpy as jnp
from jax import lax
from jax.sharding import PartitionSpec as P


def entering(part, axis, combine, identity, reverse):
    count = lax.axis_size(axis)
    place = lax.axis_index(axis)
    ahead = count - 1 - place if reverse else place
    gathered = jax.tree.map(lambda a: lax.all_gather(a, axis), part)
    state = jax.tree.map(lambda a, e: jnp.zeros_like(a) + jnp.asarray(e, a.dtype), part, identity)

    def one(hop, state):
        source = count - 1 - hop if reverse else hop
        return combine(
            state, jax.tree.map(lambda a: lax.dynamic_index_in_dim(a, source, 0, False), gathered)
        )

    return lax.fori_loop(0, ahead, one, state)


def dequantize(code_rows, scale_rows):
    row_count, col_count = code_rows.shape
    group_count = scale_rows.shape[1]
    spread = code_rows.astype(jnp.float32).reshape(row_count, group_count, col_count // group_count)
    spread = spread * scale_rows.astype(jnp.float32)[:, :, None]
    return spread.reshape(row_count, col_count).astype(jnp.bfloat16)


def block_prep(ld_block):
    cum_log = jnp.cumsum(ld_block, axis=1)
    input_scale = jnp.sqrt(-jnp.expm1(2.0 * ld_block))
    tail_weight = jnp.exp(cum_log[:, -1:] - cum_log) * input_scale
    return (cum_log, input_scale, tail_weight)


def weighted_pair(x_vals, grad_out, tail_weight, cum_log, inv_root):
    head_weight = jnp.exp(cum_log) * inv_root
    weighted_x = (x_vals.astype(jnp.float32) * tail_weight.T[:, :, None]).astype(jnp.bfloat16)
    weighted_g = (grad_out.astype(jnp.float32) * head_weight.T[:, :, None]).astype(jnp.bfloat16)
    return (weighted_x, weighted_g)


def summaries(x_vals, b_mat, c_mat, grad_out, ld_block):
    cum_log, input_scale, tail_weight = block_prep(ld_block)
    inv_root = 1.0 / math.sqrt(b_mat.shape[1])
    weighted_x, weighted_g = weighted_pair(x_vals, grad_out, tail_weight, cum_log, inv_root)
    fwd_state = jnp.einsum("sn,shp->hnp", b_mat, weighted_x, preferred_element_type=jnp.float32)
    back_state = jnp.einsum("tn,thp->hnp", c_mat, weighted_g, preferred_element_type=jnp.float32)
    return (jnp.exp(cum_log[:, -1]), fwd_state, back_state)


def block_grads(x_vals, b_mat, c_mat, grad_out, ld_block, state_in, back_in):
    block_len = ld_block.shape[1]
    cum_log, input_scale, tail_weight = block_prep(ld_block)
    inv_root = 1.0 / math.sqrt(b_mat.shape[1])
    weighted_x, weighted_g = weighted_pair(x_vals, grad_out, tail_weight, cum_log, inv_root)
    row_ids = lax.broadcasted_iota(jnp.int32, (block_len, block_len), 0)
    col_ids = lax.broadcasted_iota(jnp.int32, (block_len, block_len), 1)
    lower_mask = (row_ids >= col_ids)[None]
    log_gap = cum_log[:, :, None] - cum_log[:, None, :]
    decay_mat = jnp.where(lower_mask, jnp.exp(jnp.where(lower_mask, log_gap, 0.0)), 0.0)
    state_low = state_in.astype(jnp.bfloat16)
    back_low = back_in.astype(jnp.bfloat16)
    x_dot_g = jnp.einsum("thp,shp->hts", grad_out, x_vals, preferred_element_type=jnp.float32)
    c_dot_b = jnp.dot(c_mat, b_mat.T, preferred_element_type=jnp.float32)
    mix_weights = (
        jnp.sum(decay_mat * input_scale[:, None, :] * x_dot_g, axis=0) * inv_root
    ).astype(jnp.bfloat16)
    d_c = jnp.einsum("hnp,thp->tn", state_low, weighted_g, preferred_element_type=jnp.float32)
    d_c = d_c + jnp.dot(mix_weights, b_mat, preferred_element_type=jnp.float32)
    d_b = jnp.einsum("hnp,thp->tn", back_low, weighted_x, preferred_element_type=jnp.float32)
    d_b = d_b + jnp.dot(mix_weights.T, c_mat, preferred_element_type=jnp.float32)
    d_x = (
        jnp.einsum("tn,hnp->thp", b_mat, back_low, preferred_element_type=jnp.float32)
        * tail_weight.T[:, :, None]
    )
    inner_weights = (decay_mat * c_dot_b[None] * inv_root).astype(jnp.bfloat16)
    inner = jnp.einsum("hus,uhp->shp", inner_weights, grad_out, preferred_element_type=jnp.float32)
    d_x = d_x + input_scale.T[:, :, None] * inner
    return (d_x, d_b, d_c)


def state_chain(decays, adds, start, backward):

    def step(carry, item):
        return (item[0][:, None, None] * carry + item[1], carry)

    return lax.scan(step, start, (decays, adds), reverse=backward)


def join_summary(earlier, later):
    return (earlier[0] * later[0], later[0][:, None, None] * earlier[1] + later[1])


def local(inputs, weight_codes, scales, log_decay, cotangent):
    tok_count = inputs.shape[1]
    features = inputs[0]
    grad_out = cotangent[0]
    head_count = log_decay.shape[1]
    hp_width = grad_out.shape[1]
    head_dim = hp_width // head_count
    proj_width = weight_codes.shape[1]
    state_width = (proj_width - hp_width) // 2
    full_codes, full_scales = (
        lax.all_gather(weight_codes, "seq", axis=0, tiled=True),
        lax.all_gather(scales, "seq", axis=0, tiled=True),
    )
    weights = dequantize(full_codes, full_scales)
    projected = jnp.dot(features, weights, preferred_element_type=jnp.float32).astype(jnp.bfloat16)
    block_len = min(128, tok_count)
    block_count = tok_count // block_len
    x_blocks = projected[:, :hp_width].reshape(block_count, block_len, head_count, head_dim)
    b_blocks = projected[:, hp_width : hp_width + state_width].reshape(
        block_count, block_len, state_width
    )
    c_blocks = projected[:, hp_width + state_width :].reshape(block_count, block_len, state_width)
    g_blocks = grad_out.reshape(block_count, block_len, head_count, head_dim)
    ld_blocks = log_decay[0].reshape(head_count, block_count, block_len).transpose(1, 0, 2)
    decays, fwd_states, back_states = jax.vmap(summaries)(
        x_blocks, b_blocks, c_blocks, g_blocks, ld_blocks
    )
    zero_state = jnp.zeros((head_count, state_width, head_dim), jnp.float32)
    dev_decay = jnp.prod(decays, axis=0)
    dev_fwd, unused_a = state_chain(decays, fwd_states, zero_state, False)
    dev_back, unused_b = state_chain(decays, back_states, zero_state, True)
    neutral = (jnp.ones((head_count,), jnp.float32), zero_state)
    carried = entering((dev_decay, dev_fwd), "seq", join_summary, neutral, False)
    returned = entering((dev_decay, dev_back), "seq", join_summary, neutral, True)
    unused_c, state_starts = state_chain(decays, fwd_states, carried[1], False)
    unused_d, back_starts = state_chain(decays, back_states, returned[1], True)
    d_x, d_b, d_c = lax.map(
        lambda block_item: block_grads(*block_item),
        (x_blocks, b_blocks, c_blocks, g_blocks, ld_blocks, state_starts, back_starts),
    )
    d_proj = jnp.concatenate(
        [
            d_x.reshape(tok_count, hp_width),
            d_b.reshape(tok_count, state_width),
            d_c.reshape(tok_count, state_width),
        ],
        axis=1,
    ).astype(jnp.bfloat16)
    grad_in = lax.dot_general(
        d_proj, weights, (((1,), (1,)), ((), ())), preferred_element_type=jnp.float32
    )
    seq_count = lax.axis_size("seq")
    group_count = lax.axis_size("dp")
    norm_factor = 1.0 / math.sqrt(group_count * seq_count * tok_count)
    partial_grad = lax.psum_scatter(
        lax.dot_general(
            features, d_proj, (((0,), (0,)), ((), ())), preferred_element_type=jnp.float32
        ),
        "seq",
        scatter_dimension=0,
        tiled=True,
    )
    summed_grad = lax.psum(partial_grad, "dp")
    return (grad_in[None], summed_grad * norm_factor)


def solution(mesh):
    placed = (
        P("dp", "seq", None),
        P("seq", None),
        P("seq", None),
        P("dp", None, "seq"),
        P("dp", "seq", None),
    )
    return jax.shard_map(
        local,
        mesh=mesh,
        in_specs=placed,
        out_specs=(P("dp", "seq", None), P("seq", None)),
        check_vma=False,
    )
```

profile of v0, /device:TPU:2, one launch (start us, length us, event | category | flops | bytes accessed | tf_op | source)
XLA Modules:
  0.0 521.6 jit_solution(17085878530613788069)
XLA Ops:
  8.0 24.6 %all-gather.1 = bf16[32,64,10]{1,2,0:T(8,128)(2,1)S(1)} all-gather(bf16[1,64,10]{1,2,0:T(8,128)(2,1)} %bitcast.145), channel_id=1, replica_groups=mesh['dp'=8,'seq'=32] {'seq'}, dimensions={0}, use_global_device_ids=true | all-gather | bytes 42240 | tf_op jit(solution)/shard_map/all_gather | solution.py:109
  35.8 1.3 fusion.43
  37.1 28.6 %all-gather.6.cloned.1.call-done = bf16[2048,1280]{1,0:T(8,128)(2,1)} async-done(((bf16[64,1280]{1,0:T(8,128)(2,1)}), bf16[2048,1280]{1,0:T(8,128)(2,1)}) %all-gather.6.cloned.1.call-update) | async-done | bytes 5242896 | tf_op jit(solution)/shard_map/all_gather | solution.py:108
  65.7 7.9 %copy.59 = bf16[2048,1280]{0,1:T(8,128)(2,1)} copy(bf16[2048,1280]{1,0:T(8,128)(2,1)} %all-gather.6.cloned.1.call-done) | data formatting | bytes 10485760 | tf_op jit(solution)/shard_map/all_gather | solution.py:108
  73.6 3.9 fusion
  77.6 2.4 copy-done.2
  80.0 1.5 fusion.1
  85.5 21.4 %all-gather = f32[32,16,1]{1,2,0:T(1,128)} all-gather(f32[1,16,1]{1,2,0:T(1,128)S(1)} %exp.58), channel_id=2, replica_groups=mesh['dp'=8,'seq'=32] {'seq'}, dimensions={0}, use_global_device_ids=true | all-gather | bytes 2112 | tf_op jit(solution)/shard_map/all_gather | solution.py:12
  108.7 52.1 %all-gather.10.cloned.1.call-done = f32[32,16,128,64]{2,3,1,0:T(8,128)} async-done(((f32[1,16,128,64]{2,3,1,0:T(8,128)}), f32[32,16,128,64]{2,3,1,0:T(8,128)}) %all-gather.10.cloned.1.call-update) | async-done | bytes 16777232 | tf_op jit(solution)/shard_map/all_gather | solution.py:12
  160.9 4.7 while.17
  160.9 1.1 constant_dynamic-slice_fusion.5
  163.3 1.1 constant_dynamic-slice_fusion.5
  165.6 74.8 %all-gather.8.cloned.1.call-done = f32[32,16,128,64]{2,3,1,0:T(8,128)} async-done(((f32[1,16,128,64]{2,3,1,0:T(8,128)}), f32[32,16,128,64]{2,3,1,0:T(8,128)}) %all-gather.8.cloned.1.call-update) | async-done | bytes 16777232 | tf_op jit(solution)/shard_map/all_gather | solution.py:12
  240.5 68.7 %while.16 = (s32[]{:T(128)}, f32[16,128,64]{2,1,0:T(8,128)S(1)}, s32[]{:T(128)}, f32[32,16]{1,0:T(8,128)}, f32[32,16,128,64]{2,3,1,0:T(8,128)}, /*index=5*/s32[]{:T(128)}, s32[]{:T(128)}, s32[]{:T(128)}, s32[]{:T(128)}) while((s32[]{:T(128)}, f32[16,128,64]{2,1,0:T(8,128)S(1)}, s32[]{:T(128)}, f32[32,16]{1,0:T(8,128)}, ...), condition=%wide.region_2.3_spmd, body=%wide.region_1.2_spmd.sunk | while | flops 262150 | bytes 3670363 | solution.py:21
  240.6 1.1 constant_dynamic-slice_fusion.4
  242.9 1.1 constant_dynamic-slice_fusion.4
  245.3 1.1 constant_dynamic-slice_fusion.4
  247.7 1.1 constant_dynamic-slice_fusion.4
  250.1 1.1 constant_dynamic-slice_fusion.4
  252.4 1.1 constant_dynamic-slice_fusion.4
  254.8 1.1 constant_dynamic-slice_fusion.4
  257.2 1.1 constant_dynamic-slice_fusion.4
  259.5 1.1 constant_dynamic-slice_fusion.4
  261.9 1.1 constant_dynamic-slice_fusion.4
  264.3 1.1 constant_dynamic-slice_fusion.4
  266.6 1.1 constant_dynamic-slice_fusion.4
  269.0 1.1 constant_dynamic-slice_fusion.4
  273.7 1.1 constant_dynamic-slice_fusion.4
  276.1 1.1 constant_dynamic-slice_fusion.4
  278.4 1.1 constant_dynamic-slice_fusion.4
  283.2 1.1 constant_dynamic-slice_fusion.4
  285.6 1.1 constant_dynamic-slice_fusion.4
  290.3 1.1 constant_dynamic-slice_fusion.4
  292.7 1.1 constant_dynamic-slice_fusion.4
  297.4 1.1 constant_dynamic-slice_fusion.4
  299.8 1.1 constant_dynamic-slice_fusion.4
  302.1 1.1 constant_dynamic-slice_fusion.4
  304.5 1.1 constant_dynamic-slice_fusion.4
  306.9 1.1 constant_dynamic-slice_fusion.4
  309.6 1.2 convolution_bitcast_fusion.7
  310.8 1.5 convolution_bitcast_fusion.6
  313.5 5.3 %convolution_bitcast_fusion = f32[2048,1280]{0,1:T(8,128)} fusion(bf16[1,128,2048]{2,1,0:T(8,128)(2,1)S(1)} %copy-done, bf16[128,128]{0,1:T(8,128)(2,1)S(1)} %fusion.12, bf16[128,128]{0,1:T(8,128)(2,1)S(1)} %fusion.11, bf16[128,1024]{0,1:T(8,128)(2,1)S(1)} %bitcast.132), kind=kOutput, calls=%fused_computation.8 | convolution fusion | flops 672071680 | bytes 11337728 | tf_op jit(solution)/shard_map/dot_general | solution.py:153
  318.9 11.3 %copy.89 = f32[2048,1280]{1,0:T(8,128)} copy(f32[2048,1280]{0,1:T(8,128)} %convolution_bitcast_fusion) | data formatting | bytes 20971520
  330.2 106.7 %reduce-scatter.4.cloned.1.call-done = f32[64,1280]{1,0:T(8,128)} async-done(((f32[2048,1280]{1,0:T(8,128)}), f32[64,1280]{1,0:T(8,128)}) %reduce-scatter.4.cloned.1.call-update) | async-done | bytes 327696
  436.9 2.1 copy.90
  439.0 4.3 convolution_bitcast_fusion.1
  443.4 69.7 %all-reduce.2.cloned.1.call-done = f32[64,1280]{0,1:T(8,128)} async-done(((f32[64,1280]{0,1:T(8,128)}), f32[64,1280]{0,1:T(8,128)}) %all-reduce.2.cloned.1.call-update) | async-done | bytes 327696 | tf_op jit(solution)/shard_map/psum | solution.py:160
  513.0 1.1 broadcast_multiply_fusion
  (154 shorter events, 55.2 us)
Async XLA Ops:
  7.2 72.8 %copy-start = (bf16[1,128,2048]{2,1,0:T(8,128)(2,1)S(1)}, bf16[1,128,2048]{2,1,0:T(8,128)(2,1)}, u32[]{:S(2)}) copy-start(bf16[1,128,2048]{2,1,0:T(8,128)(2,1)} %param.9) | copy-start | bytes 1572868
  7.2 58.5 %all-gather.6.cloned.1.call-start = ((), (), s32[]{:S(2)}) async-start(), calls=%async_computation.1 | async-start | bytes 5406720 | tf_op jit(solution)/shard_map/all_gather | solution.py:108
  7.9 152.9 %all-gather.10.cloned.1.call-start = ((), (), s32[]{:S(2)}) async-start(), calls=%async_computation.3 | async-start | bytes 17301504 | tf_op jit(solution)/shard_map/all_gather | solution.py:12
  77.6 2.4 copy-start.2
  79.9 3.4 copy-start.5
  83.3 157.1 %all-gather.8.cloned.1.call-start = ((), (), s32[]{:S(2)}) async-start(), calls=%async_computation.2 | async-start | bytes 17301504 | tf_op jit(solution)/shard_map/all_gather | solution.py:12
  83.6 77.2 %copy-start.3 = (bf16[1,128,1024]{1,2,0:T(8,128)(2,1)}, bf16[1,128,1024]{1,2,0:T(8,128)(2,1)S(1)}, u32[]{:S(2)}) copy-start(bf16[1,128,1024]{1,2,0:T(8,128)(2,1)S(1)} %copy.63) | copy-start | bytes 786436
  85.4 351.5 %reduce-scatter.4.cloned.1.call-start = ((), (), s32[]{:S(2)}) async-start(), calls=%async_computation.5 | async-start | bytes 10813440
  106.9 53.9 %copy-start.7 = (pred[128,128]{0,1:T(8,128)(4,1)}, pred[128,128]{0,1:T(8,128)(4,1)S(1)}, u32[]{:S(2)}) copy-start(pred[128,128]{0,1:T(8,128)(4,1)S(1)} %iota_compare_fusion) | copy-start | bytes 49156
  165.6 74.9 %copy-start.1 = (f32[16,128,64]{2,1,0:T(8,128)}, f32[16,128,64]{2,1,0:T(8,128)S(1)}, u32[]{:S(2)}) copy-start(f32[16,128,64]{2,1,0:T(8,128)S(1)} %get-tuple-element.218) | copy-start | bytes 1572868
  309.2 3.7 copy-start.4
  309.2 3.7 copy-start.6
  309.2 3.7 copy-start.8
  309.3 3.7 copy-start.9
  330.2 182.8 %all-reduce.2.cloned.1.call-start = ((), (), s32[]{:S(2)}) async-start(), calls=%async_computation.4 | async-start | bytes 1310720 | tf_op jit(solution)/shard_map/psum | solution.py:160
Sparse Core Ops, SparseCore 0:
  10.6 55.0 all-gather.5
  83.4 77.2 all-gather.9
  163.3 77.0 all-gather.7
  330.3 106.5 reduce-scatter.3
  439.2 73.7 all-reduce.1
where the time goes:
time: 525 us; the launch traced here: 522 us
  waiting for transfers between devices  333 us (63%)
  local copies, waits for them, and re-layouts  91.1 us (17%)
  blocking collectives  46 us (9%)
  matrix products  18.9 us (4%)
  other arithmetic  17.6 us (3%)
  between operations  14 us (3%)
    all_gather x2, waiting for transfers between devices, entering(): gathered = jax.tree.map(lambda a: lax.all_gather(a, axis), part)  127 us
    unnamed x6, waiting for transfers between devices  107 us
    psum x1, waiting for transfers between devices, local(): summed_grad = lax.psum(partial_grad, 'dp')  69.7 us
    dynamic_slice x62, local copies, waits for them, and re-layouts, one(): lax.dynamic_index_in_dim(a, source, 0, False)  43.9 us
    all_gather x1, waiting for transfers between devices, local(): lax.all_gather(weight_codes, 'seq', axis=0, tiled=True)  28.6 us
    all_gather x1, blocking collectives, local(): lax.all_gather(scales, 'seq', axis=0, tiled=True)  24.6 us
    mul x31, local copies, waits for them, and re-layouts, join_summary(): later[0][:, None, None] * earlier[1] + later[1]  21.4 us
    all_gather x1, blocking collectives, entering(): gathered = jax.tree.map(lambda a: lax.all_gather(a, axis), part)  21.4 us
  transfers between devices with their start and end apart: 5, of which 5 were waited for; matrix products, arithmetic and copies ran while one was open for 3% of the time, Pallas kernels for 0%

commit v1 on v0

--- a/solution.py
+++ b/solution.py
@@ -105,7 +105,9 @@
     proj_width = weight_codes.shape[1]
     state_width = (proj_width - hp_width) // 2
     full_codes, full_scales = (
-        lax.all_gather(weight_codes, "seq", axis=0, tiled=True),
+        jnp.concatenate(
+            lax.all_to_all(jnp.stack([weight_codes] * lax.axis_size("seq")), "seq", 0, 0), axis=0
+        ),
         lax.all_gather(scales, "seq", axis=0, tiled=True),
     )
     weights = dequantize(full_codes, full_scales)

time: 525 us -> 590 us (1.12)
  waiting for transfers between devices: 333 us -> 276 us
  blocking collectives: 46 us -> 98.9 us
  local copies, waits for them, and re-layouts: 91.1 us -> 128 us
  other arithmetic: 17.6 us -> 34.5 us
  starting transfers between devices: 0.2 us -> 7.84 us
  matrix products: 18.9 us -> 25.4 us
    all_gather x2, waiting for transfers between devices: 127 us -> 61.2 us  [entering(): gathered = jax.tree.map(lambda a: lax.all_gather(a, axis), part)]
    all_gather x1, blocking collectives: 24.6 us -> 76.3 us  [local(): lax.all_gather(scales, 'seq', axis=0, tiled=True)]
    unnamed x6 -> x5, waiting for transfers between devices: 107 us -> 146 us
    all_gather x1 -> x0, waiting for transfers between devices: 28.6 us -> none  [local(): lax.all_gather(weight_codes, 'seq', axis=0, tiled=True)]
    convert_element_type x0 -> x2, local copies, waits for them, and re-layouts: none -> 23.8 us  [the longest x1 11.9 us: dequantize(): code_rows.astype(jnp.float32)]
    convert_element_type x1 -> x2, other arithmetic: 3.92 us -> 23.6 us  [dequantize(): return spread.reshape(row_count, col_count).astype(jnp.bfloat16)]
    mul x0 -> x2, local copies, waits for them, and re-layouts: none -> 16.5 us  [dequantize(): spread = spread * scale_rows.astype(jnp.float32)[:, :, None]]
    all_gather x1 -> x0, local copies, waits for them, and re-layouts: 7.95 us -> none  [local(): lax.all_gather(weight_codes, 'seq', axis=0, tiled=True)]
  transfers between devices with their start and end apart: 5 -> 5, of which waited for: 5 -> 4; matrix products, arithmetic and copies ran while one was open for 3% -> 19% of each run, Pallas kernels for 0% -> 0%
where the time goes in v1:
time: 590 us; the launch traced here: 586 us
  waiting for transfers between devices  276 us (47%)
  local copies, waits for them, and re-layouts  128 us (22%)
  blocking collectives  98.9 us (17%)
  other arithmetic  34.5 us (6%)
  matrix products  25.4 us (4%)
  between operations  14 us (2%)
  starting transfers between devices  7.84 us (1%)
    unnamed x5, waiting for transfers between devices  146 us
    all_gather x1, blocking collectives, local(): lax.all_gather(scales, 'seq', axis=0, tiled=True)  76.3 us
    psum x1, waiting for transfers between devices, local(): summed_grad = lax.psum(partial_grad, 'dp')  68.7 us
    all_gather x2, waiting for transfers between devices, entering(): gathered = jax.tree.map(lambda a: lax.all_gather(a, axis), part)  61.2 us
    dynamic_slice x62, local copies, waits for them, and re-layouts, one(): lax.dynamic_index_in_dim(a, source, 0, False)  44.4 us
    convert_element_type x2, other arithmetic, dequantize(): return spread.reshape(row_count, col_count).astype(jnp.bfloat16)  23.6 us
    all_gather x1, blocking collectives, entering(): gathered = jax.tree.map(lambda a: lax.all_gather(a, axis), part)  22.6 us
    mul x31, local copies, waits for them, and re-layouts, join_summary(): later[0][:, None, None] * earlier[1] + later[1]  21.3 us
  transfers between devices with their start and end apart: 5, of which 4 were waited for; matrix products, arithmetic and copies ran while one was open for 19% of the time, Pallas kernels for 0%

profile of v1, /device:TPU:2, one launch (start us, length us, event | category | flops | bytes accessed | tf_op | source)
XLA Modules:
  0.0 586.0 jit_solution(12791751854829433891)
XLA Ops:
  7.2 3.9 stack.2
  11.1 7.7 %all-to-all-start = ((bf16[32,64,1280]{2,1,0:T(8,128)(2,1)}), bf16[32,64,1280]{2,1,0:T(8,128)(2,1)}, u32[]{:S(2)}, u32[]{:S(2)}) async-start(bf16[32,64,1280]{2,1,0:T(8,128)(2,1)} %stack.2), calls=%async_computation | async-start | bytes 10485760 | tf_op jit(solution)/shard_map/all_to_all | solution.py:109
  19.5 76.3 %all-gather.1 = bf16[32,64,10]{1,2,0:T(8,128)(2,1)S(1)} all-gather(bf16[1,64,10]{1,2,0:T(8,128)(2,1)S(1)} %bitcast.150), channel_id=1, replica_groups=mesh['dp'=8,'seq'=32] {'seq'}, dimensions={0}, use_global_device_ids=true | all-gather | bytes 42240 | tf_op jit(solution)/shard_map/all_gather | solution.py:111
  98.2 11.9 %reshape.199 = f32[2048,10,128]{2,1,0:T(8,128)} reshape(bf16[32,64,1280]{2,1,0:T(8,128)(2,1)} %all-to-all-done) | data formatting | bytes 15728640 | tf_op jit(solution)/shard_map/convert_element_type | solution.py:27
  110.1 14.6 %multiply_convert_fusion = bf16[2048,10,128]{2,1,0:T(8,128)(2,1)} fusion(f32[2048,10,128]{2,1,0:T(8,128)} %reshape.199, f32[2048,10]{1,0:T(8,128)S(1)} %bitcast.134), kind=kLoop, calls=%fused_computation.6 | loop fusion | flops 5242880 | bytes 15810560 | tf_op jit(solution)/shard_map/convert_element_type | solution.py:29
  124.7 11.9 %copy.88 = bf16[2048,10,128]{0,2,1:T(8,128)(2,1)} copy(bf16[2048,10,128]{2,1,0:T(8,128)(2,1)} %multiply_convert_fusion) | data formatting | bytes 10485760 | tf_op jit(solution)/shard_map/convert_element_type | solution.py:29
  136.6 4.0 fusion.1
  143.6 22.6 %all-gather = f32[32,16,1]{1,2,0:T(1,128)} all-gather(f32[1,16,1]{1,2,0:T(1,128)S(1)} %exp.58), channel_id=2, replica_groups=mesh['dp'=8,'seq'=32] {'seq'}, dimensions={0}, use_global_device_ids=true | all-gather | bytes 2112 | tf_op jit(solution)/shard_map/all_gather | solution.py:12
  168.1 53.7 %all-gather.5.cloned.1.call-done = f32[32,16,128,64]{2,3,1,0:T(8,128)} async-done(((f32[1,16,128,64]{2,3,1,0:T(8,128)}), f32[32,16,128,64]{2,3,1,0:T(8,128)}) %all-gather.5.cloned.1.call-update) | async-done | bytes 16777232 | tf_op jit(solution)/shard_map/all_gather | solution.py:12
  221.9 69.2 %while.16 = (s32[]{:T(128)}, f32[16,128,64]{2,1,0:T(8,128)S(1)}, s32[]{:T(128)}, f32[32,16]{1,0:T(8,128)}, f32[32,16,128,64]{2,3,1,0:T(8,128)}, /*index=5*/s32[]{:T(128)}, s32[]{:T(128)}, s32[]{:T(128)}, s32[]{:T(128)}) while((s32[]{:T(128)}, f32[16,128,64]{2,1,0:T(8,128)S(1)}, s32[]{:T(128)}, f32[32,16]{1,0:T(8,128)}, ...), condition=%wide.region_2.3_spmd, body=%wide.region_1.2_spmd.sunk | while | flops 262150 | bytes 3670355 | solution.py:21
  224.3 1.1 constant_dynamic-slice_fusion.4
  226.7 1.1 constant_dynamic-slice_fusion.4
  229.0 1.1 constant_dynamic-slice_fusion.4
  236.1 1.1 constant_dynamic-slice_fusion.4
  240.9 1.1 constant_dynamic-slice_fusion.4
  243.3 1.1 constant_dynamic-slice_fusion.4
  245.7 1.1 constant_dynamic-slice_fusion.4
  248.1 1.1 constant_dynamic-slice_fusion.4
  250.4 1.1 constant_dynamic-slice_fusion.4
  252.8 1.1 constant_dynamic-slice_fusion.4
  260.0 1.1 constant_dynamic-slice_fusion.4
  262.3 1.2 constant_dynamic-slice_fusion.4
  264.9 1.1 constant_dynamic-slice_fusion.4
  267.2 1.1 constant_dynamic-slice_fusion.4
  269.6 1.1 constant_dynamic-slice_fusion.4
  272.0 1.2 constant_dynamic-slice_fusion.4
  274.4 1.1 constant_dynamic-slice_fusion.4
  281.5 1.1 constant_dynamic-slice_fusion.4
  283.9 1.1 constant_dynamic-slice_fusion.4
  286.3 1.1 constant_dynamic-slice_fusion.4
  288.7 1.2 constant_dynamic-slice_fusion.4
  292.1 1.9 convolution_bitcast_fusion.7
  294.0 7.5 %all-gather.7.cloned.1.call-done = f32[32,16,128,64]{2,3,1,0:T(8,128)} async-done(((f32[1,16,128,64]{2,3,1,0:T(8,128)}), f32[32,16,128,64]{2,3,1,0:T(8,128)}) %all-gather.7.cloned.1.call-update) | async-done | bytes 16777232 | tf_op jit(solution)/shard_map/all_gather | solution.py:12
  301.6 4.9 while.17
  307.5 1.2 convolution_bitcast_fusion.6
  308.9 1.2 fusion.32
  310.0 1.6 fusion.10
  311.6 5.3 convolution_bitcast_fusion
  317.0 11.3 %copy.120 = f32[2048,1280]{1,0:T(8,128)} copy(f32[2048,1280]{0,1:T(8,128)} %convolution_bitcast_fusion) | data formatting | bytes 20971520
  328.3 1.1 copy-done.2
  329.8 5.3 mul.263.clone
  335.1 11.2 %copy.106 = f32[2048,1280]{1,0:T(8,128)} copy(f32[2048,1280]{0,1:T(8,128)} %bitcast.133) | data formatting | bytes 20971520 | tf_op jit(solution)/shard_map/mul | solution.py:28
  346.3 9.0 %fusion = bf16[2048,1280]{1,0:T(8,128)(2,1)} fusion(f32[2048,1280]{1,0:T(8,128)} %copy.106, bf16[32,64,1280]{2,1,0:T(8,128)(2,1)} %all-to-all-done), kind=kLoop, calls=%fused_computation.8 | loop fusion | flops 7864320 | bytes 20971520 | tf_op jit(solution)/shard_map/convert_element_type | solution.py:29
  355.3 146.0 %reduce-scatter.4.cloned.1.call-done = f32[64,1280]{1,0:T(8,128)} async-done(((f32[2048,1280]{1,0:T(8,128)}), f32[64,1280]{1,0:T(8,128)}) %reduce-scatter.4.cloned.1.call-update) | async-done | bytes 327696
  501.2 2.1 copy.121
  503.3 5.3 convolution_bitcast_fusion.1
  508.6 68.7 %all-reduce.2.cloned.1.call-done = f32[64,1280]{0,1:T(8,128)} async-done(((f32[64,1280]{0,1:T(8,128)}), f32[64,1280]{0,1:T(8,128)}) %all-reduce.2.cloned.1.call-update) | async-done | bytes 327696 | tf_op jit(solution)/shard_map/psum | solution.py:162
  577.3 1.1 broadcast_multiply_fusion
  (155 shorter events, 60.7 us)
Async XLA Ops:
  7.2 129.4 %copy-start = (bf16[1,128,2048]{2,1,0:T(8,128)(2,1)S(1)}, bf16[1,128,2048]{2,1,0:T(8,128)(2,1)}, u32[]{:S(2)}) copy-start(bf16[1,128,2048]{2,1,0:T(8,128)(2,1)} %param.9) | copy-start | bytes 1572868
  7.2 11.6 %copy-start.5 = (f32[1,16,128]{2,1,0:T(8,128)S(1)}, f32[1,16,128]{2,1,0:T(8,128)}, u32[]{:S(2)}) copy-start(f32[1,16,128]{2,1,0:T(8,128)} %param.12) | copy-start | bytes 24580
  7.2 12.1 %copy-start.4 = (bf16[1,128,1024]{2,1,0:T(8,128)(2,1)S(1)}, bf16[1,128,1024]{2,1,0:T(8,128)(2,1)}, u32[]{:S(2)}) copy-start(bf16[1,128,1024]{2,1,0:T(8,128)(2,1)} %param.13) | copy-start | bytes 786436
  7.2 12.2 %copy-start.7 = (bf16[64,10]{0,1:T(8,128)(2,1)S(1)}, bf16[64,10]{0,1:T(8,128)(2,1)}, u32[]{:S(2)}) copy-start(bf16[64,10]{0,1:T(8,128)(2,1)} %param.11) | copy-start | bytes 3844
  11.1 87.1 %all-to-all-start = ((bf16[32,64,1280]{2,1,0:T(8,128)(2,1)}), bf16[32,64,1280]{2,1,0:T(8,128)(2,1)}, u32[]{:S(2)}, u32[]{:S(2)}) async-start(bf16[32,64,1280]{2,1,0:T(8,128)(2,1)} %stack.2), calls=%async_computation | async-start | bytes 10485760 | tf_op jit(solution)/shard_map/all_to_all | solution.py:109
  18.8 203.1 %all-gather.5.cloned.1.call-start = ((), (), s32[]{:S(2)}) async-start(), calls=%async_computation.2 | async-start | bytes 17301504 | tf_op jit(solution)/shard_map/all_gather | solution.py:12
  19.4 146.9 %copy-start.3 = (bf16[1,128,1024]{1,2,0:T(8,128)(2,1)}, bf16[1,128,1024]{1,2,0:T(8,128)(2,1)S(1)}, u32[]{:S(2)}) copy-start(bf16[1,128,1024]{1,2,0:T(8,128)(2,1)S(1)} %copy.91) | copy-start | bytes 786436
  96.2 13.9 %copy-start.1 = (f32[32,64,10]{2,1,0:T(8,128)}, f32[32,64,10]{2,1,0:T(8,128)S(1)}, u32[]{:S(2)}) copy-start(f32[32,64,10]{2,1,0:T(8,128)S(1)} %copy.115) | copy-start | bytes 245764
  141.7 159.8 %all-gather.7.cloned.1.call-start = ((), (), s32[]{:S(2)}) async-start(), calls=%async_computation.3 | async-start | bytes 17301504 | tf_op jit(solution)/shard_map/all_gather | solution.py:12
  143.6 357.7 %reduce-scatter.4.cloned.1.call-start = ((), (), s32[]{:S(2)}) async-start(), calls=%async_computation.5 | async-start | bytes 10813440
  166.3 55.6 %copy-start.6 = (pred[128,128]{0,1:T(8,128)(4,1)}, pred[128,128]{0,1:T(8,128)(4,1)S(1)}, u32[]{:S(2)}) copy-start(pred[128,128]{0,1:T(8,128)(4,1)S(1)} %iota_compare_fusion) | copy-start | bytes 49156
  328.2 1.2 copy-start.2
  328.3 249.1 %all-reduce.2.cloned.1.call-start = ((), (), s32[]{:S(2)}) async-start(), calls=%async_computation.4 | async-start | bytes 1310720 | tf_op jit(solution)/shard_map/psum | solution.py:162
Sparse Core Ops, SparseCore 0:
  141.8 79.9 all-gather.4
  224.4 77.0 all-gather.6
  328.4 172.8 reduce-scatter.3
  503.6 73.7 all-reduce.1
